TPU v7x, 256 devices: a whole 4x4x8 slice. The times are simulated.
256 devices in a mesh: node: 8 (over z_lo, core), drow: 4 (over x), dcol: 8 (over z_hi, y).
Axes of the slice: x: 4, y: 4, z: 8 (z_hi: 2, z_lo: 4; z = z_hi * 4 + z_lo), core: 2. Of those that a mesh axis runs over, the one named last changes fastest.
Arguments:
- freq_resp: bfloat16 [2, 8, 4096, 8192], P(None, None, ('drow', 'dcol'), 'node'), may hold values from -0.0625 to 0.0625
- node_coords: int32 [2, 8192], P(None, 'node'), may hold values from 0 to 1023
- heading_steps: int32 [2, 512], replicated, may hold values from -8 to 8
- spectral_weights: int32 [8, 512], replicated, may hold values from 1 to 64
Outputs:
- cross_spectra: float32 [2, 8, 4, 1024, 4096], P(None, None, 'drow', 'node', 'dcol')
All inputs are finite; a program needn't handle non-finite values.
Results may differ from a plain program's by a relative error of at most 0.0038.
Values may be sent and summed in bfloat16 or wider, within the bound.
No kernel may reach another device: no remote copies, remote signals or barrier semaphores. Data moves between devices by JAX's collectives and lax.ppermute only.
A program may use at most 128 MiB of HBM per device.

v0:
```python
import math
import jax
import jax.numpy as jnp
from jax import lax
from jax.sharding import PartitionSpec as P

DIRS = 512
FREQS = 8
GRID = 1024


def unit_phasor(turn):
    quarter = GRID // 4
    shifted = turn + quarter // 2 & GRID - 1
    quadrant = shifted >> 8
    offset = (shifted & quarter - 1) - quarter // 2
    x = offset.astype(jnp.float32) * (2.0 * math.pi / GRID)
    x2 = x * x
    s = x * (1.0 + x2 * (-1.0 / 6 + x2 * (1.0 / 120 + x2 * (-1.0 / 5040 + x2 * (1.0 / 362880)))))
    c = 1.0 + x2 * (-0.5 + x2 * (1.0 / 24 + x2 * (-1.0 / 720 + x2 * (1.0 / 40320))))
    odd = quadrant & 1 == 1
    cos_mag = jnp.where(odd, s, c)
    sin_mag = jnp.where(odd, c, s)
    cos_neg = (quadrant == 1) | (quadrant == 2)
    sin_neg = quadrant >= 2
    return (jnp.where(cos_neg, -cos_mag, cos_mag), jnp.where(sin_neg, -sin_mag, sin_mag))


def excitation(coords, heading_steps, spectral_weights):
    freq_index = (jnp.arange(FREQS, dtype=jnp.int32) + 1)[:, None, None]
    project = (
        coords[0][:, None] * heading_steps[0][None, :]
        + coords[1][:, None] * heading_steps[1][None, :]
    )
    turn_count = freq_index * project[None] & GRID - 1
    cos_t, sin_t = unit_phasor(turn_count)
    spread = jnp.sqrt(spectral_weights.astype(jnp.float32) / (64.0 * DIRS))[:, None, :]
    load_re = (spread * cos_t).astype(jnp.bfloat16)
    load_im = (-spread * sin_t).astype(jnp.bfloat16)
    return (load_re, load_im)


def local(freq_resp, node_coords, heading_steps, spectral_weights):
    load_re, load_im = excitation(node_coords, heading_steps, spectral_weights)
    right = jnp.stack(
        [
            jnp.concatenate([load_re, load_im], axis=-1),
            jnp.concatenate([-load_im, load_re], axis=-1),
        ],
        axis=0,
    )
    partial_amp = jnp.einsum("pfkn,pfne->fke", freq_resp, right, preferred_element_type=jnp.float32)
    amplitudes = lax.psum_scatter(partial_amp, "node", scatter_dimension=1, tiled=True).astype(
        jnp.bfloat16
    )
    cols = lax.all_gather(amplitudes, ("node", "drow"), axis=1, tiled=True)
    rows = lax.all_gather(amplitudes, "dcol", axis=1, tiled=True)
    rows_im = jnp.concatenate([rows[..., DIRS:], -rows[..., :DIRS]], axis=-1)
    lead = jnp.stack([rows, rows_im], axis=0)
    spec = jnp.einsum("pfke,fje->pfkj", lead, cols, preferred_element_type=jnp.float32)
    return spec[:, :, None]


def solution(mesh):
    placed = (P(None, None, ("drow", "dcol"), "node"), P(None, "node"), P(), P())
    return jax.shard_map(
        local,
        mesh=mesh,
        in_specs=placed,
        out_specs=P(None, None, "drow", "node", "dcol"),
        check_vma=False,
    )
```

profile of v0, /device:TPU:1, one launch (start us, length us, event | category | flops | bytes accessed | tf_op | source)
XLA Modules:
  0.0 358.4 jit_solution(1211883478855104320)
XLA Ops:
  6.5 0.0 reduce-scatter.2.cloned.1.call-start
  6.5 0.8 fusion.37
  7.3 0.8 fusion.36
  8.1 0.7 fusion.33
  8.8 0.4 multiply_add_fusion.1
  9.2 22.0 %fusion.34 = bf16[8,1024,512]{1,2,0:T(8,128)(2,1)} fusion(s32[1024,512]{0,1:T(8,128)S(1)} %multiply_add_fusion.1, s32[8]{0:T(128)S(1)} %iota_add_fusion, f32[8,512]{1,0:T(8,128)S(1)} %get-tuple-element.13), kind=kLoop, calls=%fused_computation.43 | loop fusion | flops 159383552 | bytes 10502176 | tf_op jit(solution)/shard_map/neg | solution.py:48
  31.2 26.0 %fusion.7 = (bf16[8,1024,512]{1,2,0:T(8,128)(2,1)}, bf16[8,1024,512]{1,2,0:T(8,128)(2,1)}) fusion(f32[8,512]{1,0:T(8,128)S(1)} %get-tuple-element.13, s32[1024,512]{0,1:T(8,128)S(1)} %multiply_add_fusion.1, s32[8]{0:T(128)S(1)} %iota_add_fusion, f32[8,512]{1,0:T(8,128)S(1)} %get-tuple-element.14), kind=kLoop, calls=%fused_computation.9 | loop fusion | flops 180355072 | bytes 18907168 | tf_op jit(solution)/shard_map/convert_element_type | solution.py:39
  57.2 24.9 %maximum_bitcast_fusion = (bf16[1,8,1024,1024]{2,3,0,1:T(8,128)(2,1)}, bf16[1,8,1024,1024]{2,3,0,1:T(8,128)(2,1)}) fusion(bf16[8,1024,512]{1,2,0:T(8,128)(2,1)} %get-tuple-element.7, bf16[8,1024,512]{1,2,0:T(8,128)(2,1)} %get-tuple-element.8, bf16[8,1024,512]{1,2,0:T(8,128)(2,1)} %fusion.34), kind=kLoop, calls=%fused_computation.10 | loop fusion | flops 67108864 | bytes 58720256 | tf_op jit(solution)/shard_map/stack | solution.py:45
  82.1 17.9 %fusion.26 = f32[8,128,1024]{1,2,0:T(8,128)} fusion(bf16[2,8,128,1024]{3,2,1,0:T(8,128)(2,1)} %param.4, bf16[1,8,1024,1024]{2,3,0,1:T(8,128)(2,1)} %get-tuple-element.6, bf16[1,8,1024,1024]{2,3,0,1:T(8,128)(2,1)} %get-tuple-element.5), kind=kOutput, calls=%fused_computation.33 | convolution fusion | flops 4311744512 | bytes 41943040 | tf_op jit(solution)/shard_map/pfkn,pfne->fke/dot_general | solution.py:52
  100.0 5.5 %copy.12 = f32[8,128,1024]{2,0,1:T(8,128)} copy(f32[8,128,1024]{1,2,0:T(8,128)} %fusion.26) | data formatting | bytes 8388608 | tf_op jit(solution)/shard_map/pfkn,pfne->fke/dot_general | solution.py:52
  105.5 0.0 reduce-scatter.2.cloned.1.call-update
  105.5 0.0 all-gather.5.cloned.1.call-start
  105.6 56.8 %reduce-scatter.2.cloned.1.call-done = f32[8,16,1024]{2,0,1:T(8,128)} async-done(((f32[8,128,1024]{2,0,1:T(8,128)}), f32[8,16,1024]{2,0,1:T(8,128)}) %reduce-scatter.2.cloned.1.call-update) | async-done | bytes 524304 | tf_op jit(solution)/shard_map/reduce_scatter | solution.py:53
  162.4 1.8 convert_element_type.19
  164.2 0.0 all-gather.5.cloned.1.call-update
  164.2 0.2 all-gather.3.cloned.1.call-start
  164.4 0.5 all-gather.3.cloned.1.call-update
  164.9 76.3 %all-gather.5.cloned.1.call-done = bf16[8,128,1024]{2,0,1:T(8,128)(2,1)} async-done(((bf16[8,16,1024]{2,0,1:T(8,128)(2,1)}), bf16[8,128,1024]{2,0,1:T(8,128)(2,1)}) %all-gather.5.cloned.1.call-update) | async-done | bytes 2097168 | tf_op jit(solution)/shard_map/all_gather | solution.py:57
  241.2 2.7 copy.32
  243.9 0.1 fusion.35
  244.1 1.6 maximum_bitcast_fusion.2
  245.6 89.8 %all-gather.3.cloned.1.call-done = bf16[8,512,1024]{2,0,1:T(8,128)(2,1)} async-done(((bf16[8,16,1024]{2,0,1:T(8,128)(2,1)}), bf16[8,512,1024]{2,0,1:T(8,128)(2,1)}) %all-gather.3.cloned.1.call-update) | async-done | bytes 8388624 | tf_op jit(solution)/shard_map/all_gather | solution.py:56
  335.5 11.0 %fusion.21 = f32[2,8,1,128,512]{3,4,0,1,2:T(8,128)} fusion(bf16[1,8,128,1024]{3,2,0,1:T(8,128)(2,1)} %maximum_bitcast_fusion.2, bf16[1,8,128,1024]{3,2,0,1:T(8,128)(2,1)S(1)} %bitcast.25, bf16[8,512,1024,1]{2,0,1,3:T(8,128)(2,1)} %bitcast.30), kind=kOutput, calls=%fused_computation.32 | convolution fusion | flops 2155872256 | bytes 16777216 | tf_op jit(solution)/shard_map/pfke,fje->pfkj/dot_general | solution.py:60
  346.5 5.3 %copy.17 = f32[2,8,1,128,512]{4,3,2,1,0:T(8,128)} copy(f32[2,8,1,128,512]{3,4,0,1,2:T(8,128)} %fusion.21) | data formatting | bytes 8388608 | tf_op jit(solution)/shard_map/broadcast_in_dim | solution.py:61
  (1 shorter events, 0.0 us)
Async XLA Ops:
  6.5 155.8 %reduce-scatter.2.cloned.1.call-start = ((), (), s32[]{:S(2)}) async-start(), calls=%async_computation.1 | async-start | bytes 4718592 | tf_op jit(solution)/shard_map/reduce_scatter | solution.py:53
  105.5 135.6 %all-gather.5.cloned.1.call-start = ((), (), s32[]{:S(2)}) async-start(), calls=%async_computation.3 | async-start | bytes 2359296 | tf_op jit(solution)/shard_map/all_gather | solution.py:57
  164.2 171.3 %all-gather.3.cloned.1.call-start = ((), (), s32[]{:S(2)}) async-start(), calls=%async_computation.2 | async-start | bytes 8650752 | tf_op jit(solution)/shard_map/all_gather | solution.py:56
Sparse Core Ops, SparseCore 0:
  105.7 56.6 reduce-scatter.1
  165.0 76.1 all-gather.4
  243.0 92.4 all-gather.2
where the time goes:
time: 359 us; the launch traced here: 358 us
  waiting for transfers between devices  223 us (62%)
  other arithmetic  77.5 us (22%)
  matrix products  28.9 us (8%)
  local copies, waits for them, and re-layouts  15.1 us (4%)
  between operations  13.1 us (4%)
    all_gather x1, waiting for transfers between devices, local(): cols = lax.all_gather(amplitudes, ('node', 'drow'), axis=1, tiled=True)  89.8 us
    all_gather x1, waiting for transfers between devices, local(): rows = lax.all_gather(amplitudes, 'dcol', axis=1, tiled=True)  76.3 us
    reduce_scatter x1, waiting for transfers between devices, local(): lax.psum_scatter(partial_amp, 'node', scatter_dimension=1, tiled=True)  56.8 us
    convert_element_type x1, other arithmetic, excitation(): load_im = (-spread * sin_t).astype(jnp.bfloat16)  26 us
    another operation x1, other arithmetic, local(): jnp.stack([jnp.concatenate([load_re, load_im], axis=-1), jnp.concatenate(...  24.9 us
    neg x1, other arithmetic, local(): -load_im  22 us
    dot_general x1, matrix products, local(): jnp.einsum('pfkn,pfne->fke', freq_resp, right, preferred_element_type=jnp...  17.9 us
    dot_general x1, matrix products, local(): jnp.einsum('pfke,fje->pfkj', lead, cols, preferred_element_type=jnp.float32)  11 us
  transfers between devices with their start and end apart: 3, of which 3 were waited for; matrix products, arithmetic and copies ran while one was open for 1% of the time, Pallas kernels for 0%

commit v1 on v0

--- a/solution.py
+++ b/solution.py
@@ -53,7 +53,12 @@
     amplitudes = lax.psum_scatter(partial_amp, "node", scatter_dimension=1, tiled=True).astype(
         jnp.bfloat16
     )
-    cols = lax.all_gather(amplitudes, ("node", "drow"), axis=1, tiled=True)
+    cols = jnp.concatenate(
+        lax.all_to_all(
+            jnp.stack([amplitudes] * lax.axis_size(("node", "drow"))), ("node", "drow"), 0, 0
+        ),
+        axis=1,
+    )
     rows = lax.all_gather(amplitudes, "dcol", axis=1, tiled=True)
     rows_im = jnp.concatenate([rows[..., DIRS:], -rows[..., :DIRS]], axis=-1)
     lead = jnp.stack([rows, rows_im], axis=0)

time: 359 us -> 422 us (1.18)
  waiting for transfers between devices: 223 us -> 268 us
  local copies, waits for them, and re-layouts: 15.1 us -> 28.2 us
  starting transfers between devices: 0.27 us -> 7.89 us
    all_to_all x0 -> x1, waiting for transfers between devices: none -> 119 us  [local(): lax.all_to_all(jnp.stack([amplitudes] * lax.axis_size(('node', 'drow'))),...]
    all_gather x1 -> x0, waiting for transfers between devices: 89.8 us -> none  [local(): cols = lax.all_gather(amplitudes, ('node', 'drow'), axis=1, tiled=True)]
    all_gather x1, waiting for transfers between devices: 76.3 us -> 91.7 us  [local(): rows = lax.all_gather(amplitudes, 'dcol', axis=1, tiled=True)]
    reshape x0 -> x1, local copies, waits for them, and re-layouts: none -> 8.68 us  [local(): jnp.concatenate(lax.all_to_all(jnp.stack([amplitudes] * lax.axis_size(('n...]
    all_to_all x0 -> x1, starting transfers between devices: none -> 7.66 us  [local(): lax.all_to_all(jnp.stack([amplitudes] * lax.axis_size(('node', 'drow'))),...]
    another operation x0 -> x1, local copies, waits for them, and re-layouts: none -> 4.3 us  [local(): jnp.stack([amplitudes] * lax.axis_size(('node', 'drow')))]
where the time goes in v1:
time: 422 us
  waiting for transfers between devices  268 us (64%)
  other arithmetic  76.7 us (18%)
  local copies, waits for them, and re-layouts  28.2 us (7%)
  matrix products  27.5 us (7%)
  between operations  13.5 us (3%)
  starting transfers between devices  7.89 us (2%)
    all_to_all x1, waiting for transfers between devices, local(): lax.all_to_all(jnp.stack([amplitudes] * lax.axis_size(('node', 'drow'))),...  119 us
    all_gather x1, waiting for transfers between devices, local(): rows = lax.all_gather(amplitudes, 'dcol', axis=1, tiled=True)  91.7 us
    reduce_scatter x1, waiting for transfers between devices, local(): lax.psum_scatter(partial_amp, 'node', scatter_dimension=1, tiled=True)  56.8 us
    convert_element_type x1, other arithmetic, excitation(): load_im = (-spread * sin_t).astype(jnp.bfloat16)  25.9 us
    another operation x1, other arithmetic, local(): jnp.stack([jnp.concatenate([load_re, load_im], axis=-1), jnp.concatenate(...  24.8 us
    neg x1, other arithmetic, local(): -load_im  22 us
    dot_general x1, matrix products, local(): jnp.einsum('pfkn,pfne->fke', freq_resp, right, preferred_element_type=jnp...  17.9 us
    dot_general x1, matrix products, local(): jnp.einsum('pfke,fje->pfkj', lead, cols, preferred_element_type=jnp.float32)  9.57 us
  transfers between devices with their start and end apart: 3, of which 3 were waited for; matrix products, arithmetic and copies ran while one was open for 1% of the time, Pallas kernels for 0%

profile of v1, /device:TPU:1, one launch (start us, length us, event | category | flops | bytes accessed | tf_op | source)
XLA Modules:
  0.0 421.5 jit_solution(7686834050441413872)
XLA Ops:
  6.5 0.8 fusion.34
  7.3 0.8 fusion.33
  8.1 0.7 fusion.30
  8.8 0.4 multiply_add_fusion.1
  9.2 22.0 %fusion.31 = bf16[8,1024,512]{1,2,0:T(8,128)(2,1)} fusion(s32[1024,512]{0,1:T(8,128)S(1)} %multiply_add_fusion.1, s32[8]{0:T(128)S(1)} %iota_add_fusion, f32[8,512]{1,0:T(8,128)S(1)} %get-tuple-element.13), kind=kLoop, calls=%fused_computation.42 | loop fusion | flops 159383552 | bytes 10502176 | tf_op jit(solution)/shard_map/neg | solution.py:48
  31.2 25.9 %fusion.7 = (bf16[8,1024,512]{1,2,0:T(8,128)(2,1)}, bf16[8,1024,512]{1,2,0:T(8,128)(2,1)}) fusion(f32[8,512]{1,0:T(8,128)S(1)} %get-tuple-element.13, s32[1024,512]{0,1:T(8,128)S(1)} %multiply_add_fusion.1, s32[8]{0:T(128)S(1)} %iota_add_fusion, f32[8,512]{1,0:T(8,128)S(1)} %get-tuple-element.14), kind=kLoop, calls=%fused_computation.9 | loop fusion | flops 180355072 | bytes 18907168 | tf_op jit(solution)/shard_map/convert_element_type | solution.py:39
  57.2 24.8 %maximum_bitcast_fusion = (bf16[1,8,1024,1024]{2,3,0,1:T(8,128)(2,1)}, bf16[1,8,1024,1024]{2,3,0,1:T(8,128)(2,1)}) fusion(bf16[8,1024,512]{1,2,0:T(8,128)(2,1)} %get-tuple-element.7, bf16[8,1024,512]{1,2,0:T(8,128)(2,1)} %get-tuple-element.8, bf16[8,1024,512]{1,2,0:T(8,128)(2,1)} %fusion.31), kind=kLoop, calls=%fused_computation.10 | loop fusion | flops 67108864 | bytes 58720256 | tf_op jit(solution)/shard_map/stack | solution.py:45
  82.0 17.9 %fusion.23 = f32[8,128,1024]{1,2,0:T(8,128)} fusion(bf16[2,8,128,1024]{3,2,1,0:T(8,128)(2,1)} %param.4, bf16[1,8,1024,1024]{2,3,0,1:T(8,128)(2,1)} %get-tuple-element.6, bf16[1,8,1024,1024]{2,3,0,1:T(8,128)(2,1)} %get-tuple-element.5), kind=kOutput, calls=%fused_computation.32 | convolution fusion | flops 4311744512 | bytes 41943040 | tf_op jit(solution)/shard_map/pfkn,pfne->fke/dot_general | solution.py:52
  99.9 5.5 %copy.12 = f32[8,128,1024]{2,0,1:T(8,128)} copy(f32[8,128,1024]{1,2,0:T(8,128)} %fusion.23) | data formatting | bytes 8388608 | tf_op jit(solution)/shard_map/pfkn,pfne->fke/dot_general | solution.py:52
  105.4 56.8 %reduce-scatter.2.cloned.1.call-done = f32[8,16,1024]{2,0,1:T(8,128)} async-done(((f32[8,128,1024]{2,0,1:T(8,128)}), f32[8,16,1024]{2,0,1:T(8,128)}) %reduce-scatter.2.cloned.1.call-update) | async-done | bytes 524304 | tf_op jit(solution)/shard_map/reduce_scatter | solution.py:53
  162.3 1.1 convert_element_type.19
  163.3 0.2 copy.13
  163.5 4.3 %stack.17 = bf16[32,8,16,1024]{3,2,1,0:T(8,128)(2,1)} broadcast(bf16[8,16,1024]{2,1,0:T(8,128)(2,1)S(1)} %copy.13), dimensions={1,2,3} | broadcast | bytes 8650752 | tf_op jit(solution)/shard_map/stack | solution.py:58
  167.8 7.7 %all-to-all-start = ((bf16[32,8,16,1024]{3,2,1,0:T(8,128)(2,1)}), bf16[32,8,16,1024]{3,2,1,0:T(8,128)(2,1)}, u32[]{:S(2)}, u32[]{:S(2)}) async-start(bf16[32,8,16,1024]{3,2,1,0:T(8,128)(2,1)} %stack.17), calls=%async_computation.1 | async-start | bytes 16777216 | tf_op jit(solution)/shard_map/all_to_all | solution.py:57
  175.5 0.2 all-gather.2.cloned.1.call-start
  175.7 0.5 all-gather.2.cloned.1.call-update
  176.2 91.7 %all-gather.2.cloned.1.call-done = bf16[8,128,1024]{2,0,1:T(8,128)(2,1)} async-done(((bf16[8,16,1024]{2,0,1:T(8,128)(2,1)}), bf16[8,128,1024]{2,0,1:T(8,128)(2,1)}) %all-gather.2.cloned.1.call-update) | async-done | bytes 2097168 | tf_op jit(solution)/shard_map/all_gather | solution.py:62
  267.9 2.7 copy.27
  270.6 0.1 fusion.32
  270.8 1.6 maximum_bitcast_fusion.2
  272.4 118.7 %all-to-all-done = bf16[32,8,16,1024]{3,2,1,0:T(8,128)(2,1)} async-done(((bf16[32,8,16,1024]{3,2,1,0:T(8,128)(2,1)}), bf16[32,8,16,1024]{3,2,1,0:T(8,128)(2,1)}, u32[]{:S(2)}, u32[]{:S(2)}) %all-to-all-start) | async-done | bytes 8388640 | tf_op jit(solution)/shard_map/all_to_all | solution.py:57
  391.1 8.7 %copy.14 = bf16[8,32,16,1024]{3,2,1,0:T(8,128)(2,1)} copy(bf16[8,32,16,1024]{3,2,0,1:T(8,128)(2,1)} %bitcast.10) | data formatting | bytes 16777216 | tf_op jit(solution)/shard_map/reshape | solution.py:56
  399.8 9.6 %fusion.20 = f32[2,8,1,128,512]{3,4,0,1,2:T(8,128)} fusion(bf16[8,512,1024,1]{2,1,3,0:T(8,128)(2,1)} %bitcast.31, bf16[1,8,128,1024]{3,2,0,1:T(8,128)(2,1)S(1)} %copy-done.1, bf16[1,8,128,1024]{3,2,0,1:T(8,128)(2,1)S(1)} %bitcast.32), kind=kOutput, calls=%fused_computation.31 | convolution fusion | flops 2155872256 | bytes 16777216 | tf_op jit(solution)/shard_map/pfke,fje->pfkj/dot_general | solution.py:65
  409.3 5.3 %copy.18 = f32[2,8,1,128,512]{4,3,2,1,0:T(8,128)} copy(f32[2,8,1,128,512]{3,4,0,1,2:T(8,128)} %fusion.20) | data formatting | bytes 8388608 | tf_op jit(solution)/shard_map/broadcast_in_dim | solution.py:66
  (7 shorter events, 0.0 us)
Async XLA Ops:
  6.5 155.7 %reduce-scatter.2.cloned.1.call-start = ((), (), s32[]{:S(2)}) async-start(), calls=%async_computation.2 | async-start | bytes 4718592 | tf_op jit(solution)/shard_map/reduce_scatter | solution.py:53
  163.3 12.4 %copy-start = (bf16[8,16,1024]{2,0,1:T(8,128)(2,1)}, bf16[8,16,1024]{2,0,1:T(8,128)(2,1)S(1)}, u32[]{:S(2)}) copy-start(bf16[8,16,1024]{2,0,1:T(8,128)(2,1)S(1)} %convert_element_type.19) | copy-start | bytes 786436
  167.8 223.3 %all-to-all-start = ((bf16[32,8,16,1024]{3,2,1,0:T(8,128)(2,1)}), bf16[32,8,16,1024]{3,2,1,0:T(8,128)(2,1)}, u32[]{:S(2)}, u32[]{:S(2)}) async-start(bf16[32,8,16,1024]{3,2,1,0:T(8,128)(2,1)} %stack.17), calls=%async_computation.1 | async-start | bytes 16777216 | tf_op jit(solution)/shard_map/all_to_all | solution.py:57
  175.5 92.4 %all-gather.2.cloned.1.call-start = ((), (), s32[]{:S(2)}) async-start(), calls=%async_computation.3 | async-start | bytes 2359296 | tf_op jit(solution)/shard_map/all_gather | solution.py:62
  391.1 8.7 %copy-start.1 = (bf16[1,8,128,1024]{3,2,0,1:T(8,128)(2,1)S(1)}, bf16[1,8,128,1024]{3,2,0,1:T(8,128)(2,1)}, u32[]{:S(2)}) copy-start(bf16[1,8,128,1024]{3,2,0,1:T(8,128)(2,1)} %maximum_bitcast_fusion.2) | copy-start | bytes 6291460
Sparse Core Ops, SparseCore 0:
  105.5 56.6 reduce-scatter.1
  178.9 88.9 all-gather.1
